TPU v7x, 128 devices: a whole 4x4x4 slice. The times are simulated.
128 devices in a mesh: row: 8 (over y, core), col: 16 (over z, x).
Axes of the slice: x: 4, y: 4, z: 4, core: 2. Of those that a mesh axis runs over, the one named last changes fastest.
Arguments:
- mock_maps: bfloat16 [1024, 163840], P('col', 'row'), may hold values from -6 to 6
- window_blocks: int32 [4], replicated, may hold values from 0 to 127, as said below
- kept_tiles: int32 [128, 4], P(('row', 'col')), may hold values from 0 to 1, as said below
- taper_index: int32 [128, 4], P(('row', 'col')), may hold values from 0 to 3, as said below
- taper_table: float32 [4], replicated, may hold values from 0.25 to 2
Outputs:
- covariance: bfloat16 [163840, 5120], P(('row', 'col'))
Inputs may be any that keep to these rules, and one draw needn't show every extreme that they name: `window_blocks`: the entries are distinct feature blocks; the first and the last feature block are always among them. `kept_tiles`: A tile whose row block is its own window column block is always kept. `taper_index`: A tile whose row block is its own window column block takes entry 0.
All inputs are finite; a program needn't handle non-finite values.
Results may differ from a plain program's by a relative error of at most 0.001.
Values may be sent and summed in bfloat16 or wider, within the bound.
No kernel may reach another device: no remote copies, remote signals or barrier semaphores. Data moves between devices by JAX's collectives and lax.ppermute only.
A program may use at most 128 MiB of HBM per device.

v0:
```python
import jax
import jax.numpy as jnp
from jax import lax
from jax.sharding import PartitionSpec as P

WINDOW = 4


def per_device(mock_maps, window_blocks, kept_tiles, taper_index, taper_table):
    block_width = mock_maps.shape[1] // lax.axis_size("col")
    local_blocks = mock_maps.shape[1] // block_width
    row = lax.axis_index("row")
    chunks = []
    for slot in range(WINDOW):
        local_id = window_blocks[slot] - row * local_blocks
        mine = (local_id >= 0) & (local_id < local_blocks)
        start = jnp.clip(local_id, 0, local_blocks - 1) * block_width
        piece = lax.dynamic_slice_in_dim(mock_maps, start, block_width, 1)
        chunks.append(jnp.where(mine, piece, jnp.zeros_like(piece)))
    local_panels = lax.psum(jnp.concatenate(chunks, axis=1), "row")
    panels = lax.all_gather(local_panels, "col", axis=0, tiled=True)
    own_block = lax.all_to_all(mock_maps, "col", split_axis=1, concat_axis=0, tiled=True)
    mock_count = own_block.shape[0]
    own_mean = jnp.sum(own_block, axis=0, dtype=jnp.float32) / mock_count
    panel_mean = jnp.sum(panels, axis=0, dtype=jnp.float32) / mock_count
    products = lax.dot_general(
        own_block, panels, (((0,), (0,)), ((), ())), preferred_element_type=jnp.float32
    )
    classes = jnp.arange(taper_table.shape[0], dtype=jnp.int32)
    weights = jnp.sum(
        jnp.where(
            classes[None, :] == taper_index[0][:, None], taper_table[None, :], jnp.float32(0.0)
        ),
        axis=1,
    )
    weight_cols = jnp.repeat(weights, block_width)
    keep_cols = jnp.repeat(kept_tiles[0], block_width)
    centred = products - mock_count * own_mean[:, None] * panel_mean[None, :]
    tile_value = weight_cols[None, :] * centred / (mock_count - 1)
    tile_value = jnp.where(keep_cols[None, :] > 0, tile_value, jnp.float32(0.0))
    return tile_value.astype(jnp.bfloat16)


def solution(mesh):
    in_specs = (P("col", "row"), P(), P(("row", "col"), None), P(("row", "col"), None), P())
    out_specs = P(("row", "col"), None)
    return jax.shard_map(
        per_device, mesh=mesh, in_specs=in_specs, out_specs=out_specs, check_vma=False
    )
```

profile of v0, /device:TPU:1, one launch (start us, length us, event | category | flops | bytes accessed | tf_op | source)
XLA Modules:
  0.0 236.2 jit_solution(14619275543654786151)
XLA Ops:
  6.5 0.0 copy-start.2
  6.5 0.0 copy-start.3
  6.5 0.0 copy-start.4
  6.5 0.0 all-reduce.2.cloned.1.call-start
  6.5 1.4 fusion.4
  10.4 1.3 dynamic-slice_select_fusion.3
  11.7 0.9 pad_maximum_fusion
  12.6 0.0 all-reduce.2.cloned.1.call-update
  12.6 0.0 all-gather.2.cloned.1.call-start
  12.7 62.7 %all-reduce.2.cloned.1.call-done = bf16[64,5120]{1,0:T(8,128)(2,1)} async-done(((bf16[64,5120]{1,0:T(8,128)(2,1)}), bf16[64,5120]{1,0:T(8,128)(2,1)}) %all-reduce.2.cloned.1.call-update) | async-done | bytes 655376 | tf_op jit(solution)/shard_map/psum | solution.py:20
  75.4 0.0 all-gather.2.cloned.1.call-update
  75.4 3.5 %copy.16 = bf16[8,16,8,1280]{3,2,0,1:T(8,128)(2,1)} copy(bf16[8,16,8,1280]{3,2,1,0:T(8,128)(2,1)} %bitcast.29) | data formatting | bytes 5242880 | tf_op jit(solution)/shard_map/all_to_all | solution.py:22
  78.9 6.7 %all-to-all-start = ((bf16[64,16,1280]{2,0,1:T(8,128)(2,1)}), bf16[64,16,1280]{2,0,1:T(8,128)(2,1)S(1)}, u32[]{:S(2)}, u32[]{:S(2)}) async-start(bf16[64,16,1280]{2,0,1:T(8,128)(2,1)} %bitcast.28), calls=%async_computation | async-start | bytes 5242880 | tf_op jit(solution)/shard_map/all_to_all | solution.py:22
  85.6 0.0 copy-done.2
  85.6 0.1 broadcast_in_dim.34
  85.7 0.0 copy-done.3
  85.7 0.0 copy-done.4
  85.7 0.2 select_reduce_fusion
  85.9 0.1 broadcast_in_dim.38
  86.0 39.3 %all-to-all-done = bf16[64,16,1280]{2,0,1:T(8,128)(2,1)S(1)} async-done(((bf16[64,16,1280]{2,0,1:T(8,128)(2,1)}), bf16[64,16,1280]{2,0,1:T(8,128)(2,1)S(1)}, u32[]{:S(2)}, u32[]{:S(2)}) %all-to-all-start) | async-done | bytes 2621472 | tf_op jit(solution)/shard_map/all_to_all | solution.py:22
  125.3 0.0 copy-start.1
  125.3 0.4 convert_reduce_fusion.1
  125.8 1.1 copy-done.1
  126.8 57.5 %all-gather.2.cloned.1.call-done = bf16[1024,5120]{1,0:T(8,128)(2,1)} async-done(((bf16[64,5120]{1,0:T(8,128)(2,1)}), bf16[1024,5120]{1,0:T(8,128)(2,1)}) %all-gather.2.cloned.1.call-update) | async-done | bytes 10485776 | tf_op jit(solution)/shard_map/all_gather | solution.py:21
  184.3 0.0 copy-start
  184.3 5.6 %convert_reduce_fusion = f32[5120]{0:T(1024)S(1)} fusion(bf16[1024,5120]{1,0:T(8,128)(2,1)} %all-gather.2.cloned.1.call-done), kind=kLoop, calls=%fused_computation.5 | loop fusion | flops 10480640 | bytes 10506240 | tf_op jit(solution)/shard_map/reduce_sum | solution.py:25
  189.9 1.3 copy-done
  191.3 20.5 %fusion.3 = bf16[1280,5120]{0,1:T(8,128)(2,1)} fusion(bf16[1024,5120]{1,0:T(8,128)(2,1)S(1)} %copy-done, bf16[1024,1280]{1,0:T(8,128)(2,1)} %bitcast.27, f32[5120]{0:T(1024)S(1)} %broadcast_multiply_fusion, f32[1280]{0:T(1024)S(1)} %convert_reduce_fusion.1, f32[5120]{0:T(1024)S(1)} %mul.45, pred[5120]{0:T(1024)(128)(4,1)S(1)} %gt.21), kind=kOutput, calls=%fused_computation.4 | convolution fusion | flops 13461094400 | bytes 26265600 | tf_op jit(solution)/shard_map/dot_general | solution.py:26
  211.7 17.6 %copy.13 = bf16[1280,5120]{1,0:T(8,128)(2,1)} copy(bf16[1280,5120]{0,1:T(8,128)(2,1)} %fusion.3) | data formatting | bytes 26214400 | tf_op jit(solution)/shard_map/convert_element_type | solution.py:41
  (4 shorter events, 0.0 us)
Async XLA Ops:
  6.5 79.1 %copy-start.2 = (s32[1,4]{1,0:T(1,128)S(1)}, s32[1,4]{1,0:T(1,128)}, u32[]{:S(2)}) copy-start(s32[1,4]{1,0:T(1,128)} %param.7) | copy-start | bytes 52
  6.5 79.2 %copy-start.3 = (f32[4]{0:T(128)S(1)}, f32[4]{0:T(128)}, u32[]{:S(2)}) copy-start(f32[4]{0:T(128)} %param.9) | copy-start | bytes 52
  6.5 79.2 %copy-start.4 = (s32[1,4]{1,0:T(1,128)S(1)}, s32[1,4]{1,0:T(1,128)}, u32[]{:S(2)}) copy-start(s32[1,4]{1,0:T(1,128)} %param.8) | copy-start | bytes 52
  6.5 68.9 %all-reduce.2.cloned.1.call-start = ((), (), s32[]{:S(2)}) async-start(), calls=%async_computation.1 | async-start | bytes 1310720 | tf_op jit(solution)/shard_map/psum | solution.py:20
  12.6 171.7 %all-gather.2.cloned.1.call-start = ((), (), s32[]{:S(2)}) async-start(), calls=%async_computation.2 | async-start | bytes 11141120 | tf_op jit(solution)/shard_map/all_gather | solution.py:21
  78.9 46.4 %all-to-all-start = ((bf16[64,16,1280]{2,0,1:T(8,128)(2,1)}), bf16[64,16,1280]{2,0,1:T(8,128)(2,1)S(1)}, u32[]{:S(2)}, u32[]{:S(2)}) async-start(bf16[64,16,1280]{2,0,1:T(8,128)(2,1)} %bitcast.28), calls=%async_computation | async-start | bytes 5242880 | tf_op jit(solution)/shard_map/all_to_all | solution.py:22
  125.3 1.5 copy-start.1
  184.3 7.0 %copy-start = (bf16[1024,5120]{1,0:T(8,128)(2,1)S(1)}, bf16[1024,5120]{1,0:T(8,128)(2,1)}, u32[]{:S(2)}) copy-start(bf16[1024,5120]{1,0:T(8,128)(2,1)} %all-gather.2.cloned.1.call-done) | copy-start | bytes 31457284
Sparse Core Ops, SparseCore 0:
  12.8 62.6 all-reduce.1
  77.5 106.7 all-gather.1
where the time goes:
time: 237 us; the launch traced here: 236 us
  waiting for transfers between devices  160 us (68%)
  local copies, waits for them, and re-layouts  25.1 us (11%)
  matrix products  20.5 us (9%)
  between operations  15.9 us (7%)
  other arithmetic  8.38 us (4%)
  starting transfers between devices  6.71 us (3%)
    psum x1, waiting for transfers between devices, per_device(): local_panels = lax.psum(jnp.concatenate(chunks, axis=1), 'row')  62.7 us
    all_gather x1, waiting for transfers between devices, per_device(): panels = lax.all_gather(local_panels, 'col', axis=0, tiled=True)  57.5 us
    all_to_all x1, waiting for transfers between devices, per_device(): lax.all_to_all(mock_maps, 'col', split_axis=1, concat_axis=0, tiled=True)  39.3 us
    dot_general x1, matrix products, per_device(): lax.dot_general(own_block, panels, (((0,), (0,)), ((), ())), preferred_el...  20.5 us
    convert_element_type x1, local copies, waits for them, and re-layouts, per_device(): return tile_value.astype(jnp.bfloat16)  17.6 us
    all_to_all x1, starting transfers between devices, per_device(): lax.all_to_all(mock_maps, 'col', split_axis=1, concat_axis=0, tiled=True)  6.66 us
    reduce_sum x1, other arithmetic, per_device(): panel_mean = jnp.sum(panels, axis=0, dtype=jnp.float32) / mock_count  5.61 us
  transfers between devices with their start and end apart: 3, of which 3 were waited for; matrix products, arithmetic and copies ran while one was open for 2% of the time, Pallas kernels for 0%

commit v1 on v0

--- a/solution.py
+++ b/solution.py
@@ -18,7 +18,25 @@
         piece = lax.dynamic_slice_in_dim(mock_maps, start, block_width, 1)
         chunks.append(jnp.where(mine, piece, jnp.zeros_like(piece)))
     local_panels = lax.psum(jnp.concatenate(chunks, axis=1), "row")
-    panels = lax.all_gather(local_panels, "col", axis=0, tiled=True)
+
+    def link_teams(mat, row_axis):
+        ndev = lax.axis_size(row_axis)
+        line_up = []
+        for num in tuple(range(ndev)):
+            line_up.append((num, (num + 1) % ndev))
+        row_list = []
+        for num in [*range(ndev)]:
+            row_list.append((num, (num - 1) % ndev))
+        current_value, kept_arr = ([mat], [mat])
+        for _ in range(ndev // 2):
+            current_value.append(lax.ppermute(current_value[-1], row_axis, line_up))
+        for _ in tuple(range((ndev - 1) // 2)):
+            prior = lax.ppermute(kept_arr[-1], row_axis, row_list)
+            kept_arr.append(prior)
+        w_next = jnp.concatenate([*current_value[::-1], *kept_arr[1:]], axis=0)
+        return jnp.roll(w_next, (lax.axis_index(row_axis) - ndev // 2) * mat.shape[0], 0)
+
+    panels = link_teams(local_panels, "col")
     own_block = lax.all_to_all(mock_maps, "col", split_axis=1, concat_axis=0, tiled=True)
     mock_count = own_block.shape[0]
     own_mean = jnp.sum(own_block, axis=0, dtype=jnp.float32) / mock_count

time: 237 us -> 359 us (1.51)
  the two profiles are of different devices: /device:TPU:1 before, /device:TPU:24 now
where the time goes in v1:
time: 359 us; the launch traced here: 357 us
  waiting for transfers between devices  183 us (51%)
  local copies, waits for them, and re-layouts  78.7 us (22%)
  starting transfers between devices  46.8 us (13%)
  matrix products  23.1 us (6%)
  between operations  16.2 us (5%)
  other arithmetic  9.55 us (3%)
    ppermute x8, waiting for transfers between devices, link_teams(): current_value.append(lax.ppermute(current_value[-1], row_axis, line_up))  68.2 us
    psum x1, waiting for transfers between devices, per_device(): local_panels = lax.psum(jnp.concatenate(chunks, axis=1), 'row')  61.5 us
    unnamed x57, local copies, waits for them, and re-layouts  55.1 us
    ppermute x7, waiting for transfers between devices, link_teams(): prior = lax.ppermute(kept_arr[-1], row_axis, row_list)  53 us
    ppermute x7, starting transfers between devices, link_teams(): prior = lax.ppermute(kept_arr[-1], row_axis, row_list)  38.6 us
    dot_general x1, matrix products, per_device(): lax.dot_general(own_block, panels, (((0,), (0,)), ((), ())), preferred_el...  23.1 us
    convert_element_type x1, local copies, waits for them, and re-layouts, per_device(): return tile_value.astype(jnp.bfloat16)  17.6 us
  transfers between devices with their start and end apart: 17, of which 10 were waited for; matrix products, arithmetic and copies ran while one was open for 10% of the time, Pallas kernels for 0%

profile of v1, /device:TPU:24, one launch (start us, length us, event | category | flops | bytes accessed | tf_op | source)
XLA Modules:
  0.0 357.1 jit_solution(2691296639391711961)
XLA Ops:
  6.5 1.5 fusion.6
  10.6 1.3 dynamic-slice_select_fusion.3
  11.9 0.9 pad_maximum_fusion
  12.8 61.5 %all-reduce.2.cloned.1.call-done = bf16[64,5120]{1,0:T(8,128)(2,1)} async-done(((bf16[64,5120]{1,0:T(8,128)(2,1)}), bf16[64,5120]{1,0:T(8,128)(2,1)}) %all-reduce.2.cloned.1.call-update) | async-done | bytes 655376 | tf_op jit(solution)/shard_map/psum | solution.py:20
  74.3 1.5 collective-permute-start
  75.8 19.6 %collective-permute-done = bf16[64,5120]{1,0:T(8,128)(2,1)S(1)} collective-permute-done((bf16[64,5120]{1,0:T(8,128)(2,1)}, bf16[64,5120]{1,0:T(8,128)(2,1)S(1)}, u32[]{:S(2)}, u32[]{:S(2)}) %collective-permute-start) | collective-permute-done | bytes 655392 | tf_op jit(solution)/shard_map/ppermute | solution.py:32
  95.4 0.9 copy-done.1
  96.3 5.3 %collective-permute-start.8 = (bf16[64,5120]{1,0:T(8,128)(2,1)}, bf16[64,5120]{1,0:T(8,128)(2,1)}, u32[]{:S(2)}, u32[]{:S(2)}) collective-permute-start(bf16[64,5120]{1,0:T(8,128)(2,1)} %all-reduce.2.cloned.1.call-done), channel_id=1, source_target_pairs={{0,15},{1,0},{2,1},{3,2},{4,3},{5,4},{6,5},{7,6},{8,7},{9,8},{10,9... | collective-permute-start | bytes 1966088 | tf_op jit(solution)/shard_map/ppermute | solution.py:34
  101.6 14.7 %collective-permute-done.1 = bf16[64,5120]{1,0:T(8,128)(2,1)S(1)} collective-permute-done((bf16[64,5120]{1,0:T(8,128)(2,1)S(1)}, bf16[64,5120]{1,0:T(8,128)(2,1)S(1)}, u32[]{:S(2)}, u32[]{:S(2)}) %collective-permute-start.1) | collective-permute-done | bytes 655392 | tf_op jit(solution)/shard_map/ppermute | solution.py:32
  116.3 0.8 copy-done.3
  117.2 5.3 %collective-permute-start.9 = (bf16[64,5120]{1,0:T(8,128)(2,1)}, bf16[64,5120]{1,0:T(8,128)(2,1)}, u32[]{:S(2)}, u32[]{:S(2)}) collective-permute-start(bf16[64,5120]{1,0:T(8,128)(2,1)} %collective-permute-done.8), channel_id=1, source_target_pairs={{0,15},{1,0},{2,1},{3,2},{4,3},{5,4},{6,5},{7,6},{8,7},{9,8},{10,9... | collective-permute-start | bytes 1966088 | tf_op jit(solution)/shard_map/ppermute | solution.py:34
  122.5 13.9 %collective-permute-done.2 = bf16[64,5120]{1,0:T(8,128)(2,1)} collective-permute-done((bf16[64,5120]{1,0:T(8,128)(2,1)S(1)}, bf16[64,5120]{1,0:T(8,128)(2,1)}, u32[]{:S(2)}, u32[]{:S(2)}) %collective-permute-start.2) | collective-permute-done | bytes 655392 | tf_op jit(solution)/shard_map/ppermute | solution.py:32
  136.4 3.5 copy.16
  139.9 6.7 %all-to-all-start = ((bf16[64,16,1280]{2,0,1:T(8,128)(2,1)}), bf16[64,16,1280]{2,0,1:T(8,128)(2,1)S(1)}, u32[]{:S(2)}, u32[]{:S(2)}) async-start(bf16[64,16,1280]{2,0,1:T(8,128)(2,1)} %bitcast.27), calls=%async_computation | async-start | bytes 5242880 | tf_op jit(solution)/shard_map/all_to_all | solution.py:40
  146.7 5.3 %collective-permute-start.10 = (bf16[64,5120]{1,0:T(8,128)(2,1)}, bf16[64,5120]{1,0:T(8,128)(2,1)S(1)}, u32[]{:S(2)}, u32[]{:S(2)}) collective-permute-start(bf16[64,5120]{1,0:T(8,128)(2,1)} %collective-permute-done.9), channel_id=1, source_target_pairs={{0,15},{1,0},{2,1},{3,2},{4,3},{5,4},{6,5},{7,6},{8,7},{9,8},{10,9... | collective-permute-start | bytes 1966088 | tf_op jit(solution)/shard_map/ppermute | solution.py:34
  152.0 18.3 %collective-permute-done.3 = bf16[64,5120]{1,0:T(8,128)(2,1)} collective-permute-done((bf16[64,5120]{1,0:T(8,128)(2,1)}, bf16[64,5120]{1,0:T(8,128)(2,1)}, u32[]{:S(2)}, u32[]{:S(2)}) %collective-permute-start.3) | collective-permute-done | bytes 655392 | tf_op jit(solution)/shard_map/ppermute | solution.py:32
  170.3 20.3 %collective-permute-done.10 = bf16[64,5120]{1,0:T(8,128)(2,1)S(1)} collective-permute-done((bf16[64,5120]{1,0:T(8,128)(2,1)}, bf16[64,5120]{1,0:T(8,128)(2,1)S(1)}, u32[]{:S(2)}, u32[]{:S(2)}) %collective-permute-start.10) | collective-permute-done | bytes 655392 | tf_op jit(solution)/shard_map/ppermute | solution.py:34
  190.6 0.9 copy-done.5
  191.5 5.1 %collective-permute-start.11 = (bf16[64,5120]{1,0:T(8,128)(2,1)S(1)}, bf16[64,5120]{1,0:T(8,128)(2,1)S(1)}, u32[]{:S(2)}, u32[]{:S(2)}) collective-permute-start(bf16[64,5120]{1,0:T(8,128)(2,1)S(1)} %collective-permute-done.10), channel_id=1, source_target_pairs={{0,15},{1,0},{2,1},{3,2},{4,3},{5,4},{6,5},{7,6},{8,7},{9,8},{10,9... | collective-permute-start | bytes 1966088 | tf_op jit(solution)/shard_map/ppermute | solution.py:34
  196.6 1.7 collective-permute-done.4
  198.3 11.3 %collective-permute-done.11 = bf16[64,5120]{1,0:T(8,128)(2,1)S(1)} collective-permute-done((bf16[64,5120]{1,0:T(8,128)(2,1)S(1)}, bf16[64,5120]{1,0:T(8,128)(2,1)S(1)}, u32[]{:S(2)}, u32[]{:S(2)}) %collective-permute-start.11) | collective-permute-done | bytes 655392 | tf_op jit(solution)/shard_map/ppermute | solution.py:34
  209.6 0.8 copy-done.7
  210.4 5.8 %collective-permute-start.12 = (bf16[64,5120]{1,0:T(8,128)(2,1)S(1)}, bf16[64,5120]{1,0:T(8,128)(2,1)}, u32[]{:S(2)}, u32[]{:S(2)}) collective-permute-start(bf16[64,5120]{1,0:T(8,128)(2,1)S(1)} %collective-permute-done.11), channel_id=1, source_target_pairs={{0,15},{1,0},{2,1},{3,2},{4,3},{5,4},{6,5},{7,6},{8,7},{9,8},{10,9... | collective-permute-start | bytes 1966088 | tf_op jit(solution)/shard_map/ppermute | solution.py:34
  216.3 12.1 %collective-permute-done.12 = bf16[64,5120]{1,0:T(8,128)(2,1)} collective-permute-done((bf16[64,5120]{1,0:T(8,128)(2,1)S(1)}, bf16[64,5120]{1,0:T(8,128)(2,1)}, u32[]{:S(2)}, u32[]{:S(2)}) %collective-permute-start.12) | collective-permute-done | bytes 655392 | tf_op jit(solution)/shard_map/ppermute | solution.py:34
  228.4 5.9 %collective-permute-start.13 = (bf16[64,5120]{1,0:T(8,128)(2,1)}, bf16[64,5120]{1,0:T(8,128)(2,1)}, u32[]{:S(2)}, u32[]{:S(2)}) collective-permute-start(bf16[64,5120]{1,0:T(8,128)(2,1)} %collective-permute-done.12), channel_id=1, source_target_pairs={{0,15},{1,0},{2,1},{3,2},{4,3},{5,4},{6,5},{7,6},{8,7},{9,8},{10,9... | collective-permute-start | bytes 1966088 | tf_op jit(solution)/shard_map/ppermute | solution.py:34
  234.3 0.9 select_reduce_fusion
  235.3 0.7 compare_bitcast_fusion
  236.5 9.3 %collective-permute-done.13 = bf16[64,5120]{1,0:T(8,128)(2,1)} collective-permute-done((bf16[64,5120]{1,0:T(8,128)(2,1)}, bf16[64,5120]{1,0:T(8,128)(2,1)}, u32[]{:S(2)}, u32[]{:S(2)}) %collective-permute-start.13) | collective-permute-done | bytes 655392 | tf_op jit(solution)/shard_map/ppermute | solution.py:34
  245.9 5.8 %collective-permute-start.14 = (bf16[64,5120]{1,0:T(8,128)(2,1)}, bf16[64,5120]{1,0:T(8,128)(2,1)S(1)}, u32[]{:S(2)}, u32[]{:S(2)}) collective-permute-start(bf16[64,5120]{1,0:T(8,128)(2,1)} %collective-permute-done.13), channel_id=1, source_target_pairs={{0,15},{1,0},{2,1},{3,2},{4,3},{5,4},{6,5},{7,6},{8,7},{9,8},{10,9... | collective-permute-start | bytes 1966088 | tf_op jit(solution)/shard_map/ppermute | solution.py:34
  251.7 2.0 constant_dynamic-update-slice_fusion.31
  253.7 2.0 constant_dynamic-update-slice_fusion.30
  255.6 2.0 constant_dynamic-update-slice_fusion.29
  257.6 2.0 constant_dynamic-update-slice_fusion.28
  259.6 2.0 constant_dynamic-update-slice_fusion.27
  261.5 2.0 constant_dynamic-update-slice_fusion.26
  263.5 2.0 constant_dynamic-update-slice_fusion.25
  265.5 2.0 constant_dynamic-update-slice_fusion.24
  267.5 0.9 constant_dynamic-update-slice_fusion.23
  268.4 2.0 constant_dynamic-update-slice_fusion.22
  270.3 2.0 constant_dynamic-update-slice_fusion.21
  272.3 2.0 constant_dynamic-update-slice_fusion.20
  274.3 2.0 constant_dynamic-update-slice_fusion.19
  276.3 2.0 constant_dynamic-update-slice_fusion.18
  278.3 2.0 constant_dynamic-update-slice_fusion.17
  280.3 0.9 constant_dynamic-update-slice_fusion.16
  281.2 2.0 constant_dynamic-update-slice_fusion.15
  283.2 2.0 constant_dynamic-update-slice_fusion.14
  285.2 0.9 constant_dynamic-update-slice_fusion.13
  286.1 0.9 constant_dynamic-update-slice_fusion.12
  287.0 2.0 constant_dynamic-update-slice_fusion.11
  289.0 2.0 constant_dynamic-update-slice_fusion.10
  290.9 0.9 constant_dynamic-update-slice_fusion.9
  291.8 0.9 constant_dynamic-update-slice_fusion.8
  292.7 0.9 constant_dynamic-update-slice_fusion.7
  293.6 2.0 constant_dynamic-update-slice_fusion.6
  295.6 2.0 constant_dynamic-update-slice_fusion.5
  297.6 0.9 constant_dynamic-update-slice_fusion.4
  298.5 0.9 constant_dynamic-update-slice_fusion.3
  299.3 2.0 constant_dynamic-update-slice_fusion.2
  301.3 2.0 constant_dynamic-update-slice_fusion.1
  303.3 0.9 constant_dynamic-update-slice_fusion
  304.2 5.4 %convert_reduce_fusion = f32[5120]{0:T(1024)S(1)} fusion(bf16[2048,5120]{1,0:T(8,128)(2,1)} %constant_dynamic-update-slice_fusion, s32[]{:T(128)S(6)} %select_n.73), kind=kLoop, calls=%fused_computation.5 | loop fusion | flops 10480640 | bytes 10506244 | tf_op jit(solution)/shard_map/reduce_sum | solution.py:43
  309.6 23.1 %fusion.3 = bf16[1280,5120]{0,1:T(8,128)(2,1)} fusion(bf16[1024,1280]{1,0:T(8,128)(2,1)S(1)} %bitcast.26, f32[5120]{0:T(1024)S(1)} %broadcast_multiply_fusion, f32[1280]{0:T(1024)S(1)} %convert_reduce_fusion.1, f32[5120]{0:T(1024)S(1)} %mul.48, pred[5120]{0:T(1024)(128)(4,1)S(1)} %gt.21, bf16[2048,5120]{1,0:T(8,128)(2,1)} %constant_dynamic-update-slice_fusion, ...), kind=kOutput, calls=%fused_computation.4 | convolution fusion | flops 13461094400 | bytes 26265604 | tf_op jit(solution)/shard_map/dot_general | solution.py:44
  332.7 17.6 %copy.13 = bf16[1280,5120]{1,0:T(8,128)(2,1)} copy(bf16[1280,5120]{0,1:T(8,128)(2,1)} %fusion.3) | data formatting | bytes 26214400 | tf_op jit(solution)/shard_map/convert_element_type | solution.py:59
  (44 shorter events, 0.7 us)
Async XLA Ops:
  6.5 67.8 %all-reduce.2.cloned.1.call-start = ((), (), s32[]{:S(2)}) async-start(), calls=%async_computation.1 | async-start | bytes 1310720 | tf_op jit(solution)/shard_map/psum | solution.py:20
  74.3 193.1 %copy-start = (bf16[64,5120]{1,0:T(8,128)(2,1)S(1)}, bf16[64,5120]{1,0:T(8,128)(2,1)}, u32[]{:S(2)}) copy-start(bf16[64,5120]{1,0:T(8,128)(2,1)} %all-reduce.2.cloned.1.call-done) | copy-start | bytes 1966084
  74.3 21.1 %collective-permute-start = (bf16[64,5120]{1,0:T(8,128)(2,1)}, bf16[64,5120]{1,0:T(8,128)(2,1)S(1)}, u32[]{:S(2)}, u32[]{:S(2)}) collective-permute-start(bf16[64,5120]{1,0:T(8,128)(2,1)} %all-reduce.2.cloned.1.call-done), channel_id=1, source_target_pairs={{0,1},{1,2},{2,3},{3,4},{4,5},{5,6},{6,7},{7,8},{8,9},{9,10},{10,1... | collective-permute-start | bytes 1966088 | tf_op jit(solution)/shard_map/ppermute | solution.py:32
  95.4 0.9 copy-start.1
  96.3 20.0 %collective-permute-start.1 = (bf16[64,5120]{1,0:T(8,128)(2,1)S(1)}, bf16[64,5120]{1,0:T(8,128)(2,1)S(1)}, u32[]{:S(2)}, u32[]{:S(2)}) collective-permute-start(bf16[64,5120]{1,0:T(8,128)(2,1)S(1)} %collective-permute-done), channel_id=1, source_target_pairs={{0,1},{1,2},{2,3},{3,4},{4,5},{5,6},{6,7},{7,8},{8,9},{9,10},{10,1... | collective-permute-start | bytes 1966088 | tf_op jit(solution)/shard_map/ppermute | solution.py:32
  96.3 20.9 %collective-permute-start.8 = (bf16[64,5120]{1,0:T(8,128)(2,1)}, bf16[64,5120]{1,0:T(8,128)(2,1)}, u32[]{:S(2)}, u32[]{:S(2)}) collective-permute-start(bf16[64,5120]{1,0:T(8,128)(2,1)} %all-reduce.2.cloned.1.call-done), channel_id=1, source_target_pairs={{0,15},{1,0},{2,1},{3,2},{4,3},{5,4},{6,5},{7,6},{8,7},{9,8},{10,9... | collective-permute-start | bytes 1966088 | tf_op jit(solution)/shard_map/ppermute | solution.py:34
  116.3 0.9 copy-start.3
  117.2 19.3 %collective-permute-start.2 = (bf16[64,5120]{1,0:T(8,128)(2,1)S(1)}, bf16[64,5120]{1,0:T(8,128)(2,1)}, u32[]{:S(2)}, u32[]{:S(2)}) collective-permute-start(bf16[64,5120]{1,0:T(8,128)(2,1)S(1)} %collective-permute-done.1), channel_id=1, source_target_pairs={{0,1},{1,2},{2,3},{3,4},{4,5},{5,6},{6,7},{7,8},{8,9},{9,10},{10,1... | collective-permute-start | bytes 1966088 | tf_op jit(solution)/shard_map/ppermute | solution.py:32
  117.2 29.5 %collective-permute-start.9 = (bf16[64,5120]{1,0:T(8,128)(2,1)}, bf16[64,5120]{1,0:T(8,128)(2,1)}, u32[]{:S(2)}, u32[]{:S(2)}) collective-permute-start(bf16[64,5120]{1,0:T(8,128)(2,1)} %collective-permute-done.8), channel_id=1, source_target_pairs={{0,15},{1,0},{2,1},{3,2},{4,3},{5,4},{6,5},{7,6},{8,7},{9,8},{10,9... | collective-permute-start | bytes 1966088 | tf_op jit(solution)/shard_map/ppermute | solution.py:34
  136.4 33.9 %collective-permute-start.3 = (bf16[64,5120]{1,0:T(8,128)(2,1)}, bf16[64,5120]{1,0:T(8,128)(2,1)}, u32[]{:S(2)}, u32[]{:S(2)}) collective-permute-start(bf16[64,5120]{1,0:T(8,128)(2,1)} %collective-permute-done.2), channel_id=1, source_target_pairs={{0,1},{1,2},{2,3},{3,4},{4,5},{5,6},{6,7},{7,8},{8,9},{9,10},{10,1... | collective-permute-start | bytes 1966088 | tf_op jit(solution)/shard_map/ppermute | solution.py:32
  139.9 96.1 %all-to-all-start = ((bf16[64,16,1280]{2,0,1:T(8,128)(2,1)}), bf16[64,16,1280]{2,0,1:T(8,128)(2,1)S(1)}, u32[]{:S(2)}, u32[]{:S(2)}) async-start(bf16[64,16,1280]{2,0,1:T(8,128)(2,1)} %bitcast.27), calls=%async_computation | async-start | bytes 5242880 | tf_op jit(solution)/shard_map/all_to_all | solution.py:40
  146.7 44.0 %collective-permute-start.10 = (bf16[64,5120]{1,0:T(8,128)(2,1)}, bf16[64,5120]{1,0:T(8,128)(2,1)S(1)}, u32[]{:S(2)}, u32[]{:S(2)}) collective-permute-start(bf16[64,5120]{1,0:T(8,128)(2,1)} %collective-permute-done.9), channel_id=1, source_target_pairs={{0,15},{1,0},{2,1},{3,2},{4,3},{5,4},{6,5},{7,6},{8,7},{9,8},{10,9... | collective-permute-start | bytes 1966088 | tf_op jit(solution)/shard_map/ppermute | solution.py:34
  170.3 28.0 %collective-permute-start.4 = (bf16[64,5120]{1,0:T(8,128)(2,1)}, bf16[64,5120]{1,0:T(8,128)(2,1)S(1)}, u32[]{:S(2)}, u32[]{:S(2)}) collective-permute-start(bf16[64,5120]{1,0:T(8,128)(2,1)} %collective-permute-done.3), channel_id=1, source_target_pairs={{0,1},{1,2},{2,3},{3,4},{4,5},{5,6},{6,7},{7,8},{8,9},{9,10},{10,1... | collective-permute-start | bytes 1966088 | tf_op jit(solution)/shard_map/ppermute | solution.py:32
  190.6 0.9 copy-start.5
  191.5 18.1 %collective-permute-start.11 = (bf16[64,5120]{1,0:T(8,128)(2,1)S(1)}, bf16[64,5120]{1,0:T(8,128)(2,1)S(1)}, u32[]{:S(2)}, u32[]{:S(2)}) collective-permute-start(bf16[64,5120]{1,0:T(8,128)(2,1)S(1)} %collective-permute-done.10), channel_id=1, source_target_pairs={{0,15},{1,0},{2,1},{3,2},{4,3},{5,4},{6,5},{7,6},{8,7},{9,8},{10,9... | collective-permute-start | bytes 1966088 | tf_op jit(solution)/shard_map/ppermute | solution.py:34
  198.3 30.0 %copy-start.9 = (bf16[64,5120]{1,0:T(8,128)(2,1)}, bf16[64,5120]{1,0:T(8,128)(2,1)S(1)}, u32[]{:S(2)}) copy-start(bf16[64,5120]{1,0:T(8,128)(2,1)S(1)} %collective-permute-done.4) | copy-start | bytes 1966084
  198.3 17.9 %collective-permute-start.5 = (bf16[64,5120]{1,0:T(8,128)(2,1)S(1)}, bf16[64,5120]{1,0:T(8,128)(2,1)S(1)}, u32[]{:S(2)}, u32[]{:S(2)}) collective-permute-start(bf16[64,5120]{1,0:T(8,128)(2,1)S(1)} %collective-permute-done.4), channel_id=1, source_target_pairs={{0,1},{1,2},{2,3},{3,4},{4,5},{5,6},{6,7},{7,8},{8,9},{9,10},{10,1... | collective-permute-start | bytes 1966088 | tf_op jit(solution)/shard_map/ppermute | solution.py:32
  209.6 0.8 copy-start.7
  210.4 17.9 %collective-permute-start.12 = (bf16[64,5120]{1,0:T(8,128)(2,1)S(1)}, bf16[64,5120]{1,0:T(8,128)(2,1)}, u32[]{:S(2)}, u32[]{:S(2)}) collective-permute-start(bf16[64,5120]{1,0:T(8,128)(2,1)S(1)} %collective-permute-done.11), channel_id=1, source_target_pairs={{0,15},{1,0},{2,1},{3,2},{4,3},{5,4},{6,5},{7,6},{8,7},{9,8},{10,9... | collective-permute-start | bytes 1966088 | tf_op jit(solution)/shard_map/ppermute | solution.py:34
  216.3 18.0 %copy-start.11 = (bf16[64,5120]{1,0:T(8,128)(2,1)}, bf16[64,5120]{1,0:T(8,128)(2,1)S(1)}, u32[]{:S(2)}) copy-start(bf16[64,5120]{1,0:T(8,128)(2,1)S(1)} %collective-permute-done.5) | copy-start | bytes 1966084
  216.3 18.0 %collective-permute-start.6 = (bf16[64,5120]{1,0:T(8,128)(2,1)S(1)}, bf16[64,5120]{1,0:T(8,128)(2,1)}, u32[]{:S(2)}, u32[]{:S(2)}) collective-permute-start(bf16[64,5120]{1,0:T(8,128)(2,1)S(1)} %collective-permute-done.5), channel_id=1, source_target_pairs={{0,1},{1,2},{2,3},{3,4},{4,5},{5,6},{6,7},{7,8},{8,9},{9,10},{10,1... | collective-permute-start | bytes 1966088 | tf_op jit(solution)/shard_map/ppermute | solution.py:32
  228.4 17.5 %collective-permute-start.13 = (bf16[64,5120]{1,0:T(8,128)(2,1)}, bf16[64,5120]{1,0:T(8,128)(2,1)}, u32[]{:S(2)}, u32[]{:S(2)}) collective-permute-start(bf16[64,5120]{1,0:T(8,128)(2,1)} %collective-permute-done.12), channel_id=1, source_target_pairs={{0,15},{1,0},{2,1},{3,2},{4,3},{5,4},{6,5},{7,6},{8,7},{9,8},{10,9... | collective-permute-start | bytes 1966088 | tf_op jit(solution)/shard_map/ppermute | solution.py:34
  234.3 17.4 %collective-permute-start.7 = (bf16[64,5120]{1,0:T(8,128)(2,1)}, bf16[64,5120]{1,0:T(8,128)(2,1)}, u32[]{:S(2)}, u32[]{:S(2)}) collective-permute-start(bf16[64,5120]{1,0:T(8,128)(2,1)} %collective-permute-done.6), channel_id=1, source_target_pairs={{0,1},{1,2},{2,3},{3,4},{4,5},{5,6},{6,7},{7,8},{8,9},{9,10},{10,1... | collective-permute-start | bytes 1966088 | tf_op jit(solution)/shard_map/ppermute | solution.py:32
  236.0 49.1 %copy-start.12 = (bf16[64,5120]{1,0:T(8,128)(2,1)S(1)}, bf16[64,5120]{1,0:T(8,128)(2,1)}, u32[]{:S(2)}) copy-start(bf16[64,5120]{1,0:T(8,128)(2,1)} %copy-done.11) | copy-start | bytes 1966084
  236.0 50.0 %copy-start.10 = (bf16[64,5120]{1,0:T(8,128)(2,1)S(1)}, bf16[64,5120]{1,0:T(8,128)(2,1)}, u32[]{:S(2)}) copy-start(bf16[64,5120]{1,0:T(8,128)(2,1)} %copy-done.9) | copy-start | bytes 1966084
  236.0 54.9 %copy-start.4 = (bf16[64,5120]{1,0:T(8,128)(2,1)S(1)}, bf16[64,5120]{1,0:T(8,128)(2,1)}, u32[]{:S(2)}) copy-start(bf16[64,5120]{1,0:T(8,128)(2,1)} %copy-done.3) | copy-start | bytes 1966084
  236.1 55.7 %copy-start.2 = (bf16[64,5120]{1,0:T(8,128)(2,1)S(1)}, bf16[64,5120]{1,0:T(8,128)(2,1)}, u32[]{:S(2)}) copy-start(bf16[64,5120]{1,0:T(8,128)(2,1)} %copy-done.1) | copy-start | bytes 1966084
  236.1 61.5 %copy-start.6 = (bf16[64,5120]{1,0:T(8,128)(2,1)S(1)}, bf16[64,5120]{1,0:T(8,128)(2,1)}, u32[]{:S(2)}) copy-start(bf16[64,5120]{1,0:T(8,128)(2,1)} %copy-done.5) | copy-start | bytes 1966084
  236.1 62.4 %copy-start.8 = (bf16[64,5120]{1,0:T(8,128)(2,1)S(1)}, bf16[64,5120]{1,0:T(8,128)(2,1)}, u32[]{:S(2)}) copy-start(bf16[64,5120]{1,0:T(8,128)(2,1)} %copy-done.7) | copy-start | bytes 1966084
  245.9 34.5 %collective-permute-start.14 = (bf16[64,5120]{1,0:T(8,128)(2,1)}, bf16[64,5120]{1,0:T(8,128)(2,1)S(1)}, u32[]{:S(2)}, u32[]{:S(2)}) collective-permute-start(bf16[64,5120]{1,0:T(8,128)(2,1)} %collective-permute-done.13), channel_id=1, source_target_pairs={{0,15},{1,0},{2,1},{3,2},{4,3},{5,4},{6,5},{7,6},{8,7},{9,8},{10,9... | collective-permute-start | bytes 1966088 | tf_op jit(solution)/shard_map/ppermute | solution.py:34
Sparse Core Ops, SparseCore 0:
  13.0 61.3 all-reduce.1
